TPU v7x, 128 devices: a whole 4x4x4 slice. The times are simulated.
128 devices in a mesh: pr: 8 (over z, core), pc: 16 (over y, x).
Axes of the slice: x: 4, y: 4, z: 4, core: 2. Of those that a mesh axis runs over, the one named last changes fastest.
Arguments:
- test_points: bfloat16 [131072, 512], P('pr'), may hold values from -15 to 15
- panel_points: bfloat16 [1024, 512], P('pc'), may hold values from -15 to 15
- factor_rows: float32 [1024, 32768], P('pc', 'pr'), may hold values from -0.03125 to 0.03125
- alpha_below: float32 [32768, 128], P(('pr', 'pc')), may hold values from -6 to 6
- targets: float32 [1024, 128], P('pc'), may hold values from -6 to 6
- inverse_block: float32 [1024, 1024], P('pc'), may hold values from -0.008 to 0.08, as said below
- predictions_in: float32 [131072, 128], P(('pr', 'pc')), may hold values from -6 to 6
Outputs:
- predictions: float32 [131072, 128], P(('pr', 'pc'))
Inputs may be any that keep to these rules, and one draw needn't show every extreme that they name: `inverse_block`: lower triangular with a positive diagonal.
All inputs are finite; a program needn't handle non-finite values.
Results may differ from a plain program's by a relative error of at most 0.0003.
Values may be sent and summed in bfloat16 or wider, within the bound.
No kernel may reach another device: no remote copies, remote signals or barrier semaphores. Data moves between devices by JAX's collectives and lax.ppermute only.
A program may use at most 128 MiB of HBM per device.

v0:
```python
import math
import jax
import jax.numpy as jnp
from jax import lax
from jax.sharding import PartitionSpec as P

LAYERS = 4
bias_var = 0.1
weight_var = 2.0


def arc_kernel(panel, test, test_norms):
    width = panel.shape[1]
    cross = jnp.dot(panel, test.T, preferred_element_type=jnp.float32) / width
    panel_var = jnp.einsum("pd,pd->p", panel, panel, preferred_element_type=jnp.float32) / width
    kern = bias_var + weight_var * cross
    panel_k = bias_var + weight_var * panel_var
    test_k = bias_var + weight_var * (test_norms / width)
    for level in range(LAYERS):
        spread = jnp.sqrt(panel_k[:, None] * test_k[None, :])
        cosine = kern / spread
        theta = jnp.arccos(cosine)
        kern = bias_var + weight_var / (2.0 * math.pi) * spread * (
            jnp.sqrt(1.0 - cosine * cosine) + (math.pi - theta) * cosine
        )
        panel_k = bias_var + 0.5 * weight_var * panel_k
        test_k = bias_var + 0.5 * weight_var * test_k
    return kern


def contract_rows(left, right):
    return lax.dot_general(
        left,
        right,
        (((0,), (0,)), ((), ())),
        precision=lax.Precision.HIGHEST,
        preferred_element_type=jnp.float32,
    )


def body(
    test_points, panel_points, factor_rows, alpha_below, targets, inverse_block, predictions_in
):
    rows = predictions_in.shape[0]
    own = lax.axis_index("pc")
    partial_sum = jnp.dot(
        factor_rows,
        lax.all_gather(alpha_below, "pc", axis=0, tiled=True),
        precision=lax.Precision.HIGHEST,
        preferred_element_type=jnp.float32,
    )
    carried = lax.psum(partial_sum, "pr")
    residual = targets - carried
    alpha_panel = lax.psum(contract_rows(inverse_block, residual), "pc")
    panel_all = lax.all_gather(panel_points, "pc", axis=0, tiled=True)
    test_own = lax.dynamic_slice_in_dim(test_points, own * rows, rows, 0)
    test_norms = jnp.einsum("nd,nd->n", test_own, test_own, preferred_element_type=jnp.float32)
    kern = lax.optimization_barrier(arc_kernel(panel_all, test_own, test_norms))
    update = contract_rows(kern, alpha_panel)
    return predictions_in + update


def solution(mesh):
    placed = (
        P("pr", None),
        P("pc", None),
        P("pc", "pr"),
        P(("pr", "pc"), None),
        P("pc", None),
        P("pc", None),
        P(("pr", "pc"), None),
    )
    return jax.shard_map(
        body, mesh=mesh, in_specs=placed, out_specs=P(("pr", "pc"), None), check_vma=False
    )
```

profile of v0, /device:TPU:0, one launch (start us, length us, event | category | flops | bytes accessed | tf_op | source)
XLA Modules:
  0.0 224.8 jit_solution(2418785735525503081)
XLA Ops:
  6.5 0.0 copy-start
  6.5 0.0 copy-start.3
  6.5 0.0 copy-start.4
  6.5 0.0 all-gather.3.cloned.1.call-start
  6.5 0.7 all-gather.3.cloned.1.call-update
  7.3 0.0 all-gather.5.cloned.1.call-start
  7.3 0.7 all-gather.5.cloned.1.call-update
  8.0 0.0 all-reduce.2.cloned.1.call-start
  8.1 1.5 fusion
  9.6 44.7 %all-gather.3.cloned.1.call-done = bf16[1024,512]{1,0:T(8,128)(2,1)} async-done(((bf16[64,512]{1,0:T(8,128)(2,1)}), bf16[1024,512]{1,0:T(8,128)(2,1)}) %all-gather.3.cloned.1.call-update) | async-done | bytes 1048592 | tf_op jit(solution)/shard_map/all_gather | solution.py:55
  54.3 0.0 copy-start.1
  54.3 1.6 fusion.1
  55.9 44.7 %all-gather.5.cloned.1.call-done = f32[4096,128]{1,0:T(8,128)} async-done(((f32[256,128]{1,0:T(8,128)}), f32[4096,128]{1,0:T(8,128)}) %all-gather.5.cloned.1.call-update) | async-done | bytes 2097168 | tf_op jit(solution)/shard_map/all_gather | solution.py:48
  100.6 0.0 copy-done
  100.6 3.0 %fusion.5 = f32[64,128]{1,0:T(8,128)S(1)} fusion(f32[64,4096]{1,0:T(8,128)S(1)} %copy-done, f32[4096,128]{1,0:T(8,128)} %all-gather.5.cloned.1.call-done), kind=kOutput, calls=%fused_computation.19 | convolution fusion | flops 402653184 | bytes 3178496 | tf_op jit(solution)/shard_map/dot_general | solution.py:46
  103.6 24.3 %psum.14 = f32[64,128]{1,0:T(8,128)S(1)} all-reduce(f32[64,128]{1,0:T(8,128)S(1)} %fusion.5), channel_id=1, replica_groups=mesh['pr'=8,'pc'=16] {'pr'}, use_global_device_ids=true, to_apply=%region_0.0 | all-reduce | flops 8192 | bytes 65536 | tf_op jit(solution)/shard_map/psum | solution.py:52
  127.9 0.0 copy-done.3
  127.9 0.0 copy-done.4
  127.9 1.4 convolution_bitcast_fusion
  129.3 0.0 all-reduce.2.cloned.1.call-update
  129.3 0.0 copy-done.1
  129.4 0.0 copy-start.2
  129.4 50.0 %multiply_add_fusion = f32[1024,1024]{0,1:T(8,128)} fusion(bf16[1024,512]{1,0:T(8,128)(2,1)S(1)} %copy-done.1, f32[1024]{0:T(1024)S(1)} %get-tuple-element.12, f32[1024]{0:T(1024)S(1)} %get-tuple-element.8, f32[1024]{0:T(1024)S(1)} %get-tuple-element.11, f32[1024]{0:T(1024)S(1)} %get-tuple-element.7, f32[1024]{0:T(1024)S(1)} %get-tuple-element.10, ...), kind=kOutput, calls=%fused_computation.1 | convolution fusion | flops 1130364928 | bytes 6324228 | tf_op jit(solution)/shard_map/dot_general | solution.py:14
  179.3 32.4 %all-reduce.2.cloned.1.call-done = f32[1024,128]{0,1:T(8,128)} async-done(((f32[1024,128]{0,1:T(8,128)}), f32[1024,128]{0,1:T(8,128)}) %all-reduce.2.cloned.1.call-update) | async-done | bytes 524304 | tf_op jit(solution)/shard_map/psum | solution.py:54
  211.7 0.0 copy-done.2
  211.7 6.5 %convolution_add_fusion = f32[1024,128]{1,0:T(8,128)} fusion(f32[1024,128]{1,0:T(8,128)S(1)} %copy-done.2, f32[1024,1024]{0,1:T(8,128)} %multiply_add_fusion, f32[1024,128]{0,1:T(8,128)} %all-reduce.2.cloned.1.call-done), kind=kOutput, calls=%fused_computation.6 | convolution fusion | flops 1610743808 | bytes 5767168 | tf_op jit(solution)/shard_map/dot_general | solution.py:32
  (2 shorter events, 0.0 us)
Async XLA Ops:
  6.5 94.1 %copy-start = (f32[64,4096]{1,0:T(8,128)S(1)}, f32[64,4096]{1,0:T(8,128)}, u32[]{:S(2)}) copy-start(f32[64,4096]{1,0:T(8,128)} %param.9) | copy-start | bytes 3145732
  6.5 121.4 %copy-start.3 = (f32[64,1024]{1,0:T(8,128)S(1)}, f32[64,1024]{1,0:T(8,128)}, u32[]{:S(2)}) copy-start(f32[64,1024]{1,0:T(8,128)} %param.12) | copy-start | bytes 786436
  6.5 121.4 %copy-start.4 = (f32[64,128]{1,0:T(8,128)S(1)}, f32[64,128]{1,0:T(8,128)}, u32[]{:S(2)}) copy-start(f32[64,128]{1,0:T(8,128)} %param.11) | copy-start | bytes 98308
  6.5 47.8 %all-gather.3.cloned.1.call-start = ((), (), s32[]{:S(2)}) async-start(), calls=%async_computation | async-start | bytes 1114112 | tf_op jit(solution)/shard_map/all_gather | solution.py:55
  7.3 93.4 %all-gather.5.cloned.1.call-start = ((), (), s32[]{:S(2)}) async-start(), calls=%async_computation.1 | async-start | bytes 2228224 | tf_op jit(solution)/shard_map/all_gather | solution.py:48
  8.0 203.7 %all-reduce.2.cloned.1.call-start = ((), (), s32[]{:S(2)}) async-start(), calls=%async_computation.2 | async-start | bytes 1048576 | tf_op jit(solution)/shard_map/psum | solution.py:54
  54.3 75.0 %copy-start.1 = (bf16[1024,512]{1,0:T(8,128)(2,1)S(1)}, bf16[1024,512]{1,0:T(8,128)(2,1)}, u32[]{:S(2)}) copy-start(bf16[1024,512]{1,0:T(8,128)(2,1)} %all-gather.3.cloned.1.call-done) | copy-start | bytes 3145732
  129.4 82.4 %copy-start.2 = (f32[1024,128]{1,0:T(8,128)S(1)}, f32[1024,128]{1,0:T(8,128)}, u32[]{:S(2)}) copy-start(f32[1024,128]{1,0:T(8,128)} %param.13) | copy-start | bytes 1572868
Sparse Core Ops, SparseCore 0:
  9.5 44.8 all-gather.2
  56.5 44.1 all-gather.4
  129.5 82.2 all-reduce.1
where the time goes:
time: 225 us
  waiting for transfers between devices  123 us (55%)
  matrix products  60.9 us (27%)
  blocking collectives  24.3 us (11%)
  between operations  13.2 us (6%)
  other arithmetic  3.1 us (1%)
    dot_general x1, matrix products, arc_kernel(): cross = jnp.dot(panel, test.T, preferred_element_type=jnp.float32) / width  50 us
    all_gather x1, waiting for transfers between devices, body(): panel_all = lax.all_gather(panel_points, 'pc', axis=0, tiled=True)  44.7 us
    all_gather x1, waiting for transfers between devices, body(): lax.all_gather(alpha_below, 'pc', axis=0, tiled=True)  44.7 us
    psum x1, waiting for transfers between devices, body(): alpha_panel = lax.psum(contract_rows(inverse_block, residual), 'pc')  32.4 us
    psum x1, blocking collectives, body(): carried = lax.psum(partial_sum, 'pr')  24.3 us
    dot_general x2, matrix products, contract_rows(): lax.dot_general(left, right, (((0,), (0,)), ((), ())), precision=lax.Prec...  7.94 us
  transfers between devices with their start and end apart: 3, of which 3 were waited for; matrix products, arithmetic and copies ran while one was open for 24% of the time, Pallas kernels for 0%

commit v1 on v0

--- a/solution.py
+++ b/solution.py
@@ -52,7 +52,21 @@
     carried = lax.psum(partial_sum, "pr")
     residual = targets - carried
     alpha_panel = lax.psum(contract_rows(inverse_block, residual), "pc")
-    panel_all = lax.all_gather(panel_points, "pc", axis=0, tiled=True)
+    ways, here, step = (lax.axis_size("pc"), lax.axis_index("pc"), panel_points.shape[0])
+    dims = [n * ways if d == 0 else n for d, n in enumerate(panel_points.shape)]
+    full = lax.dynamic_update_slice_in_dim(
+        jnp.zeros(dims, panel_points.dtype), panel_points, here * step, axis=0
+    )
+    going_up = going_down = panel_points
+    for far in range(1, ways // 2 + 1):
+        going_up = lax.ppermute(going_up, "pc", [(d, (d + 1) % ways) for d in range(ways)])
+        full = lax.dynamic_update_slice_in_dim(full, going_up, (here - far) % ways * step, axis=0)
+        if 2 * far < ways:
+            going_down = lax.ppermute(going_down, "pc", [(d, (d - 1) % ways) for d in range(ways)])
+            full = lax.dynamic_update_slice_in_dim(
+                full, going_down, (here + far) % ways * step, axis=0
+            )
+    panel_all = full
     test_own = lax.dynamic_slice_in_dim(test_points, own * rows, rows, 0)
     test_norms = jnp.einsum("nd,nd->n", test_own, test_own, preferred_element_type=jnp.float32)
     kern = lax.optimization_barrier(arc_kernel(panel_all, test_own, test_norms))

time: 225 us -> 202 us (0.90)
  waiting for transfers between devices: 123 us -> 56.3 us
  starting transfers between devices: 0.08 us -> 39.5 us
  matrix products: 60.9 us -> 64.4 us
    all_gather x1 -> x0, waiting for transfers between devices: 44.7 us -> none  [body(): panel_all = lax.all_gather(panel_points, 'pc', axis=0, tiled=True)]
    all_gather x1, waiting for transfers between devices: 44.7 us -> 0.02 us  [body(): lax.all_gather(alpha_below, 'pc', axis=0, tiled=True)]
    ppermute x0 -> x15, starting transfers between devices: none -> 39.5 us  [the longest x7 39.4 us: body(): lax.ppermute(going_down, 'pc', [(d, (d - 1) % ways) for d in range(ways)])]
    ppermute x0 -> x15, waiting for transfers between devices: none -> 26.9 us  [the longest x8 20.3 us: body(): lax.ppermute(going_up, 'pc', [(d, (d + 1) % ways) for d in range(ways)])]
    psum x1, waiting for transfers between devices: 32.4 us -> 28.7 us  [body(): alpha_panel = lax.psum(contract_rows(inverse_block, residual), 'pc')]
    dot_general x2, matrix products: 7.94 us -> 11.2 us  [contract_rows(): lax.dot_general(left, right, (((0,), (0,)), ((), ())), precision=lax.Prec...]
  transfers between devices with their start and end apart: 3 -> 17, of which waited for: 3 -> 13; matrix products, arithmetic and copies ran while one was open for 24% -> 26% of each run, Pallas kernels for 0% -> 0%
where the time goes in v1:
time: 202 us; the launch traced here: 201 us
  matrix products  64.4 us (32%)
  waiting for transfers between devices  56.3 us (28%)
  starting transfers between devices  39.5 us (20%)
  blocking collectives  24.7 us (12%)
  between operations  13.6 us (7%)
    dot_general x1, matrix products, arc_kernel(): cross = jnp.dot(panel, test.T, preferred_element_type=jnp.float32) / width  50.3 us
    ppermute x7, starting transfers between devices, body(): lax.ppermute(going_down, 'pc', [(d, (d - 1) % ways) for d in range(ways)])  39.4 us
    psum x1, waiting for transfers between devices, body(): alpha_panel = lax.psum(contract_rows(inverse_block, residual), 'pc')  28.7 us
    psum x1, blocking collectives, body(): carried = lax.psum(partial_sum, 'pr')  24.7 us
    ppermute x8, waiting for transfers between devices, body(): lax.ppermute(going_up, 'pc', [(d, (d + 1) % ways) for d in range(ways)])  20.3 us
    dot_general x2, matrix products, contract_rows(): lax.dot_general(left, right, (((0,), (0,)), ((), ())), precision=lax.Prec...  11.2 us
    ppermute x7, waiting for transfers between devices, body(): lax.ppermute(going_down, 'pc', [(d, (d - 1) % ways) for d in range(ways)])  6.62 us
  transfers between devices with their start and end apart: 17, of which 13 were waited for; matrix products, arithmetic and copies ran while one was open for 26% of the time, Pallas kernels for 0%

profile of v1, /device:TPU:0, one launch (start us, length us, event | category | flops | bytes accessed | tf_op | source)
XLA Modules:
  0.0 201.4 jit_solution(9588055798101494730)
XLA Ops:
  6.5 0.7 all-gather.2.cloned.1.call-update
  7.3 0.0 all-reduce.2.cloned.1.call-start
  7.3 5.4 %collective-permute-start.1 = (bf16[64,512]{1,0:T(8,128)(2,1)}, bf16[64,512]{1,0:T(8,128)(2,1)S(1)}, u32[]{:S(2)}, u32[]{:S(2)}) collective-permute-start(bf16[64,512]{1,0:T(8,128)(2,1)} %param.8), channel_id=1, source_target_pairs={{0,15},{1,0},{2,1},{3,2},{4,3},{5,4},{6,5},{7,6},{8,7},{9,8},{10,9... | collective-permute-start | bytes 196616 | tf_op jit(solution)/shard_map/ppermute | solution.py:65
  12.7 1.5 fusion
  14.3 0.1 broadcast_in_dim.2
  14.3 0.9 constant_dynamic-update-slice_fusion.15
  15.2 5.4 %collective-permute-start.3 = (bf16[64,512]{1,0:T(8,128)(2,1)S(1)}, bf16[64,512]{1,0:T(8,128)(2,1)S(1)}, u32[]{:S(2)}, u32[]{:S(2)}) collective-permute-start(bf16[64,512]{1,0:T(8,128)(2,1)S(1)} %collective-permute-done.1), channel_id=1, source_target_pairs={{0,15},{1,0},{2,1},{3,2},{4,3},{5,4},{6,5},{7,6},{8,7},{9,8},{10,9... | collective-permute-start | bytes 196616 | tf_op jit(solution)/shard_map/ppermute | solution.py:65
  20.6 1.9 collective-permute-done.3
  22.5 5.7 %collective-permute-start.5 = (bf16[64,512]{1,0:T(8,128)(2,1)S(1)}, bf16[64,512]{1,0:T(8,128)(2,1)S(1)}, u32[]{:S(2)}, u32[]{:S(2)}) collective-permute-start(bf16[64,512]{1,0:T(8,128)(2,1)S(1)} %collective-permute-done.3), channel_id=1, source_target_pairs={{0,15},{1,0},{2,1},{3,2},{4,3},{5,4},{6,5},{7,6},{8,7},{9,8},{10,9... | collective-permute-start | bytes 196616 | tf_op jit(solution)/shard_map/ppermute | solution.py:65
  28.2 0.5 collective-permute-done.2
  28.7 1.4 collective-permute-done.5
  30.1 5.7 %collective-permute-start.7 = (bf16[64,512]{1,0:T(8,128)(2,1)S(1)}, bf16[64,512]{1,0:T(8,128)(2,1)S(1)}, u32[]{:S(2)}, u32[]{:S(2)}) collective-permute-start(bf16[64,512]{1,0:T(8,128)(2,1)S(1)} %collective-permute-done.5), channel_id=1, source_target_pairs={{0,15},{1,0},{2,1},{3,2},{4,3},{5,4},{6,5},{7,6},{8,7},{9,8},{10,9... | collective-permute-start | bytes 196616 | tf_op jit(solution)/shard_map/ppermute | solution.py:65
  35.8 0.7 collective-permute-done.4
  36.5 1.2 collective-permute-done.7
  37.7 5.7 %collective-permute-start.9 = (bf16[64,512]{1,0:T(8,128)(2,1)S(1)}, bf16[64,512]{1,0:T(8,128)(2,1)S(1)}, u32[]{:S(2)}, u32[]{:S(2)}) collective-permute-start(bf16[64,512]{1,0:T(8,128)(2,1)S(1)} %collective-permute-done.7), channel_id=1, source_target_pairs={{0,15},{1,0},{2,1},{3,2},{4,3},{5,4},{6,5},{7,6},{8,7},{9,8},{10,9... | collective-permute-start | bytes 196616 | tf_op jit(solution)/shard_map/ppermute | solution.py:65
  43.4 0.7 collective-permute-done.6
  44.1 1.2 collective-permute-done.9
  45.3 5.8 %collective-permute-start.11 = (bf16[64,512]{1,0:T(8,128)(2,1)S(1)}, bf16[64,512]{1,0:T(8,128)(2,1)S(1)}, u32[]{:S(2)}, u32[]{:S(2)}) collective-permute-start(bf16[64,512]{1,0:T(8,128)(2,1)S(1)} %collective-permute-done.9), channel_id=1, source_target_pairs={{0,15},{1,0},{2,1},{3,2},{4,3},{5,4},{6,5},{7,6},{8,7},{9,8},{10,9... | collective-permute-start | bytes 196616 | tf_op jit(solution)/shard_map/ppermute | solution.py:65
  51.1 2.6 %collective-permute-done.8 = bf16[64,512]{1,0:T(8,128)(2,1)S(1)} collective-permute-done((bf16[64,512]{1,0:T(8,128)(2,1)S(1)}, bf16[64,512]{1,0:T(8,128)(2,1)S(1)}, u32[]{:S(2)}, u32[]{:S(2)}) %collective-permute-start.8) | collective-permute-done | bytes 65568 | tf_op jit(solution)/shard_map/ppermute | solution.py:62
  53.7 1.1 collective-permute-done.11
  54.7 5.8 %collective-permute-start.13 = (bf16[64,512]{1,0:T(8,128)(2,1)S(1)}, bf16[64,512]{1,0:T(8,128)(2,1)S(1)}, u32[]{:S(2)}, u32[]{:S(2)}) collective-permute-start(bf16[64,512]{1,0:T(8,128)(2,1)S(1)} %collective-permute-done.11), channel_id=1, source_target_pairs={{0,15},{1,0},{2,1},{3,2},{4,3},{5,4},{6,5},{7,6},{8,7},{9,8},{10,9... | collective-permute-start | bytes 196616 | tf_op jit(solution)/shard_map/ppermute | solution.py:65
  60.5 0.7 collective-permute-done.10
  61.3 7.6 %collective-permute-done.12 = bf16[64,512]{1,0:T(8,128)(2,1)S(1)} collective-permute-done((bf16[64,512]{1,0:T(8,128)(2,1)S(1)}, bf16[64,512]{1,0:T(8,128)(2,1)S(1)}, u32[]{:S(2)}, u32[]{:S(2)}) %collective-permute-start.12) | collective-permute-done | bytes 65568 | tf_op jit(solution)/shard_map/ppermute | solution.py:62
  68.9 7.5 %collective-permute-done.14 = bf16[64,512]{1,0:T(8,128)(2,1)S(1)} collective-permute-done((bf16[64,512]{1,0:T(8,128)(2,1)S(1)}, bf16[64,512]{1,0:T(8,128)(2,1)S(1)}, u32[]{:S(2)}, u32[]{:S(2)}) %collective-permute-start.14) | collective-permute-done | bytes 65568 | tf_op jit(solution)/shard_map/ppermute | solution.py:62
  76.4 0.3 fusion.1
  76.7 0.0 all-gather.2.cloned.1.call-done
  76.8 3.0 %fusion.5 = f32[64,128]{1,0:T(8,128)S(1)} fusion(f32[64,4096]{1,0:T(8,128)S(1)} %copy-done, f32[4096,128]{1,0:T(8,128)} %all-gather.2.cloned.1.call-done), kind=kOutput, calls=%fused_computation.34 | convolution fusion | flops 402653184 | bytes 3178496 | tf_op jit(solution)/shard_map/dot_general | solution.py:46
  79.7 24.7 %psum.14 = f32[64,128]{1,0:T(8,128)S(1)} all-reduce(f32[64,128]{1,0:T(8,128)S(1)} %fusion.5), channel_id=1, replica_groups=mesh['pr'=8,'pc'=16] {'pr'}, use_global_device_ids=true, to_apply=%region_0.0 | all-reduce | flops 8192 | bytes 65536 | tf_op jit(solution)/shard_map/psum | solution.py:52
  104.4 1.4 convolution_bitcast_fusion
  105.9 50.3 %multiply_add_fusion = f32[1024,1024]{1,0:T(8,128)} fusion(bf16[1024,512]{1,0:T(8,128)(2,1)S(1)} %constant_dynamic-update-slice_fusion, f32[1024]{0:T(1024)S(1)} %get-tuple-element.12, f32[1024]{0:T(1024)S(1)} %get-tuple-element.8, f32[1024]{0:T(1024)S(1)} %get-tuple-element.11, f32[1024]{0:T(1024)S(1)} %get-tuple-element.7, f32[1024]{0:T(1024)S(1)} %get-tuple-element.10, ...), kind=kOutput, calls=%fused_computation | convolution fusion | flops 1130364928 | bytes 6324228 | tf_op jit(solution)/shard_map/dot_general | solution.py:14
  156.1 28.7 %all-reduce.2.cloned.1.call-done = f32[1024,128]{0,1:T(8,128)} async-done(((f32[1024,128]{0,1:T(8,128)}), f32[1024,128]{0,1:T(8,128)}) %all-reduce.2.cloned.1.call-update) | async-done | bytes 524304 | tf_op jit(solution)/shard_map/psum | solution.py:54
  184.8 9.8 %convolution_add_fusion = f32[1024,128]{1,0:T(8,128)} fusion(f32[1024,128]{1,0:T(8,128)S(1)} %copy-done.1, f32[1024,1024]{1,0:T(8,128)} %multiply_add_fusion, f32[1024,128]{0,1:T(8,128)} %all-reduce.2.cloned.1.call-done), kind=kOutput, calls=%fused_computation.5 | convolution fusion | flops 1610743808 | bytes 5767168 | tf_op jit(solution)/shard_map/dot_general | solution.py:32
  (38 shorter events, 0.2 us)
Async XLA Ops:
  6.5 70.2 %copy-start = (f32[64,4096]{1,0:T(8,128)S(1)}, f32[64,4096]{1,0:T(8,128)}, u32[]{:S(2)}) copy-start(f32[64,4096]{1,0:T(8,128)} %param.9) | copy-start | bytes 3145732
  6.5 70.2 %all-gather.2.cloned.1.call-start = ((), (), s32[]{:S(2)}) async-start(), calls=%async_computation | async-start | bytes 2228224 | tf_op jit(solution)/shard_map/all_gather | solution.py:48
  7.3 177.6 %all-reduce.2.cloned.1.call-start = ((), (), s32[]{:S(2)}) async-start(), calls=%async_computation.1 | async-start | bytes 1048576 | tf_op jit(solution)/shard_map/psum | solution.py:54
  7.3 7.9 %collective-permute-start.1 = (bf16[64,512]{1,0:T(8,128)(2,1)}, bf16[64,512]{1,0:T(8,128)(2,1)S(1)}, u32[]{:S(2)}, u32[]{:S(2)}) collective-permute-start(bf16[64,512]{1,0:T(8,128)(2,1)} %param.8), channel_id=1, source_target_pairs={{0,15},{1,0},{2,1},{3,2},{4,3},{5,4},{6,5},{7,6},{8,7},{9,8},{10,9... | collective-permute-start | bytes 196616 | tf_op jit(solution)/shard_map/ppermute | solution.py:65
  12.7 7.9 %collective-permute-start = (bf16[64,512]{1,0:T(8,128)(2,1)}, bf16[64,512]{1,0:T(8,128)(2,1)S(1)}, u32[]{:S(2)}, u32[]{:S(2)}) collective-permute-start(bf16[64,512]{1,0:T(8,128)(2,1)} %param.8), channel_id=1, source_target_pairs={{0,1},{1,2},{2,3},{3,4},{4,5},{5,6},{6,7},{7,8},{8,9},{9,10},{10,1... | collective-permute-start | bytes 196616 | tf_op jit(solution)/shard_map/ppermute | solution.py:62
  12.7 91.7 %copy-start.2 = (f32[64,1024]{1,0:T(8,128)S(1)}, f32[64,1024]{1,0:T(8,128)}, u32[]{:S(2)}) copy-start(f32[64,1024]{1,0:T(8,128)} %param.12) | copy-start | bytes 786436
  12.7 91.7 %copy-start.3 = (f32[64,128]{1,0:T(8,128)S(1)}, f32[64,128]{1,0:T(8,128)}, u32[]{:S(2)}) copy-start(f32[64,128]{1,0:T(8,128)} %param.11) | copy-start | bytes 98308
  15.2 7.3 %collective-permute-start.3 = (bf16[64,512]{1,0:T(8,128)(2,1)S(1)}, bf16[64,512]{1,0:T(8,128)(2,1)S(1)}, u32[]{:S(2)}, u32[]{:S(2)}) collective-permute-start(bf16[64,512]{1,0:T(8,128)(2,1)S(1)} %collective-permute-done.1), channel_id=1, source_target_pairs={{0,15},{1,0},{2,1},{3,2},{4,3},{5,4},{6,5},{7,6},{8,7},{9,8},{10,9... | collective-permute-start | bytes 196616 | tf_op jit(solution)/shard_map/ppermute | solution.py:65
  20.6 8.1 %collective-permute-start.2 = (bf16[64,512]{1,0:T(8,128)(2,1)S(1)}, bf16[64,512]{1,0:T(8,128)(2,1)S(1)}, u32[]{:S(2)}, u32[]{:S(2)}) collective-permute-start(bf16[64,512]{1,0:T(8,128)(2,1)S(1)} %collective-permute-done), channel_id=1, source_target_pairs={{0,1},{1,2},{2,3},{3,4},{4,5},{5,6},{6,7},{7,8},{8,9},{9,10},{10,1... | collective-permute-start | bytes 196616 | tf_op jit(solution)/shard_map/ppermute | solution.py:62
  22.5 7.6 %collective-permute-start.5 = (bf16[64,512]{1,0:T(8,128)(2,1)S(1)}, bf16[64,512]{1,0:T(8,128)(2,1)S(1)}, u32[]{:S(2)}, u32[]{:S(2)}) collective-permute-start(bf16[64,512]{1,0:T(8,128)(2,1)S(1)} %collective-permute-done.3), channel_id=1, source_target_pairs={{0,15},{1,0},{2,1},{3,2},{4,3},{5,4},{6,5},{7,6},{8,7},{9,8},{10,9... | collective-permute-start | bytes 196616 | tf_op jit(solution)/shard_map/ppermute | solution.py:65
  28.7 7.8 %collective-permute-start.4 = (bf16[64,512]{1,0:T(8,128)(2,1)S(1)}, bf16[64,512]{1,0:T(8,128)(2,1)S(1)}, u32[]{:S(2)}, u32[]{:S(2)}) collective-permute-start(bf16[64,512]{1,0:T(8,128)(2,1)S(1)} %collective-permute-done.2), channel_id=1, source_target_pairs={{0,1},{1,2},{2,3},{3,4},{4,5},{5,6},{6,7},{7,8},{8,9},{9,10},{10,1... | collective-permute-start | bytes 196616 | tf_op jit(solution)/shard_map/ppermute | solution.py:62
  30.1 7.6 %collective-permute-start.7 = (bf16[64,512]{1,0:T(8,128)(2,1)S(1)}, bf16[64,512]{1,0:T(8,128)(2,1)S(1)}, u32[]{:S(2)}, u32[]{:S(2)}) collective-permute-start(bf16[64,512]{1,0:T(8,128)(2,1)S(1)} %collective-permute-done.5), channel_id=1, source_target_pairs={{0,15},{1,0},{2,1},{3,2},{4,3},{5,4},{6,5},{7,6},{8,7},{9,8},{10,9... | collective-permute-start | bytes 196616 | tf_op jit(solution)/shard_map/ppermute | solution.py:65
  36.5 7.6 %collective-permute-start.6 = (bf16[64,512]{1,0:T(8,128)(2,1)S(1)}, bf16[64,512]{1,0:T(8,128)(2,1)S(1)}, u32[]{:S(2)}, u32[]{:S(2)}) collective-permute-start(bf16[64,512]{1,0:T(8,128)(2,1)S(1)} %collective-permute-done.4), channel_id=1, source_target_pairs={{0,1},{1,2},{2,3},{3,4},{4,5},{5,6},{6,7},{7,8},{8,9},{9,10},{10,1... | collective-permute-start | bytes 196616 | tf_op jit(solution)/shard_map/ppermute | solution.py:62
  37.7 7.6 %collective-permute-start.9 = (bf16[64,512]{1,0:T(8,128)(2,1)S(1)}, bf16[64,512]{1,0:T(8,128)(2,1)S(1)}, u32[]{:S(2)}, u32[]{:S(2)}) collective-permute-start(bf16[64,512]{1,0:T(8,128)(2,1)S(1)} %collective-permute-done.7), channel_id=1, source_target_pairs={{0,15},{1,0},{2,1},{3,2},{4,3},{5,4},{6,5},{7,6},{8,7},{9,8},{10,9... | collective-permute-start | bytes 196616 | tf_op jit(solution)/shard_map/ppermute | solution.py:65
  44.1 9.6 %collective-permute-start.8 = (bf16[64,512]{1,0:T(8,128)(2,1)S(1)}, bf16[64,512]{1,0:T(8,128)(2,1)S(1)}, u32[]{:S(2)}, u32[]{:S(2)}) collective-permute-start(bf16[64,512]{1,0:T(8,128)(2,1)S(1)} %collective-permute-done.6), channel_id=1, source_target_pairs={{0,1},{1,2},{2,3},{3,4},{4,5},{5,6},{6,7},{7,8},{8,9},{9,10},{10,1... | collective-permute-start | bytes 196616 | tf_op jit(solution)/shard_map/ppermute | solution.py:62
  45.3 9.4 %collective-permute-start.11 = (bf16[64,512]{1,0:T(8,128)(2,1)S(1)}, bf16[64,512]{1,0:T(8,128)(2,1)S(1)}, u32[]{:S(2)}, u32[]{:S(2)}) collective-permute-start(bf16[64,512]{1,0:T(8,128)(2,1)S(1)} %collective-permute-done.9), channel_id=1, source_target_pairs={{0,15},{1,0},{2,1},{3,2},{4,3},{5,4},{6,5},{7,6},{8,7},{9,8},{10,9... | collective-permute-start | bytes 196616 | tf_op jit(solution)/shard_map/ppermute | solution.py:65
  53.7 7.6 %collective-permute-start.10 = (bf16[64,512]{1,0:T(8,128)(2,1)S(1)}, bf16[64,512]{1,0:T(8,128)(2,1)S(1)}, u32[]{:S(2)}, u32[]{:S(2)}) collective-permute-start(bf16[64,512]{1,0:T(8,128)(2,1)S(1)} %collective-permute-done.8), channel_id=1, source_target_pairs={{0,1},{1,2},{2,3},{3,4},{4,5},{5,6},{6,7},{7,8},{8,9},{9,10},{10,1... | collective-permute-start | bytes 196616 | tf_op jit(solution)/shard_map/ppermute | solution.py:62
  54.7 14.1 %collective-permute-start.13 = (bf16[64,512]{1,0:T(8,128)(2,1)S(1)}, bf16[64,512]{1,0:T(8,128)(2,1)S(1)}, u32[]{:S(2)}, u32[]{:S(2)}) collective-permute-start(bf16[64,512]{1,0:T(8,128)(2,1)S(1)} %collective-permute-done.11), channel_id=1, source_target_pairs={{0,15},{1,0},{2,1},{3,2},{4,3},{5,4},{6,5},{7,6},{8,7},{9,8},{10,9... | collective-permute-start | bytes 196616 | tf_op jit(solution)/shard_map/ppermute | solution.py:65
  61.2 7.6 %collective-permute-start.12 = (bf16[64,512]{1,0:T(8,128)(2,1)S(1)}, bf16[64,512]{1,0:T(8,128)(2,1)S(1)}, u32[]{:S(2)}, u32[]{:S(2)}) collective-permute-start(bf16[64,512]{1,0:T(8,128)(2,1)S(1)} %collective-permute-done.10), channel_id=1, source_target_pairs={{0,1},{1,2},{2,3},{3,4},{4,5},{5,6},{6,7},{7,8},{8,9},{9,10},{10,1... | collective-permute-start | bytes 196616 | tf_op jit(solution)/shard_map/ppermute | solution.py:62
  68.8 7.6 %collective-permute-start.14 = (bf16[64,512]{1,0:T(8,128)(2,1)S(1)}, bf16[64,512]{1,0:T(8,128)(2,1)S(1)}, u32[]{:S(2)}, u32[]{:S(2)}) collective-permute-start(bf16[64,512]{1,0:T(8,128)(2,1)S(1)} %collective-permute-done.12), channel_id=1, source_target_pairs={{0,1},{1,2},{2,3},{3,4},{4,5},{5,6},{6,7},{7,8},{8,9},{9,10},{10,1... | collective-permute-start | bytes 196616 | tf_op jit(solution)/shard_map/ppermute | solution.py:62
  105.9 78.9 %copy-start.1 = (f32[1024,128]{1,0:T(8,128)S(1)}, f32[1024,128]{1,0:T(8,128)}, u32[]{:S(2)}) copy-start(f32[1024,128]{1,0:T(8,128)} %param.13) | copy-start | bytes 1572868
Sparse Core Ops, SparseCore 0:
  9.5 48.2 all-gather.1
  106.0 78.7 all-reduce.1
